TPU v7x, 256 devices: a whole 4x4x8 slice. The times are simulated.
256 devices in a mesh: dp: 64 (over z, y, core), mp: 4 (over x).
Axes of the slice: x: 4, y: 4, z: 8, core: 2. Of those that a mesh axis runs over, the one named last changes fastest.
Arguments:
- acts: bfloat16 [114688, 768], P('dp'), may hold values from -250 to 250
- proj_cotangent: bfloat16 [114688, 3352], P('dp', 'mp'), may hold values from -6 to 6
- inner_acts: bfloat16 [114688, 1536], P('dp', 'mp'), may hold values from -6 to 6
- out_cotangent: bfloat16 [114688, 768], P('dp'), may hold values from -6 to 6
- in_master: float32 [768, 3352], P('dp', 'mp'), may hold values from -0.21875 to 0.21875
- in_first: float32 [768, 3352], P('dp', 'mp'), may hold values from -0.0029296875 to 0.0029296875
- in_second: float32 [768, 3352], P('dp', 'mp'), may hold values from 1e-08 to 1e-06
- out_master: float32 [1536, 768], P('mp', 'dp'), may hold values from -0.15625 to 0.15625
- out_first: float32 [1536, 768], P('mp', 'dp'), may hold values from -0.0029296875 to 0.0029296875
- out_second: float32 [1536, 768], P('mp', 'dp'), may hold values from 1e-08 to 1e-06
- conv_grads: float32 [64, 2, 5, 1792], P('dp', None, None, 'mp'), may hold values from -1800 to 1800
- conv_master: float32 [5, 1792], P(None, 'mp'), may hold values from -3 to 3
- conv_first: float32 [5, 1792], P(None, 'mp'), may hold values from -0.0029296875 to 0.0029296875
- conv_second: float32 [5, 1792], P(None, 'mp'), may hold values from 1e-06 to 0.01
- head_grads: float32 [64, 2, 24, 67], P('dp', None, 'mp'), may hold values from -1800 to 1800
- head_master: float32 [24, 67], P('mp'), may hold values from 0.5 to 2
- head_first: float32 [24, 67], P('mp'), may hold values from -0.0029296875 to 0.0029296875
- head_second: float32 [24, 67], P('mp'), may hold values from 1e-06 to 0.01
- gain_grads: float32 [64, 2, 4, 768], P('dp', None, 'mp'), may hold values from -1800 to 1800
- gain_master: float32 [768], replicated, may hold values from 0.5 to 1.5
- gain_first: float32 [768], replicated, may hold values from -0.0029296875 to 0.0029296875
- gain_second: float32 [768], replicated, may hold values from 1e-06 to 0.01
Outputs:
- in_master_new: float32 [768, 3352], P('dp', 'mp')
- in_first_new: float32 [768, 3352], P('dp', 'mp')
- in_second_new: float32 [768, 3352], P('dp', 'mp')
- in_weights: bfloat16 [768, 3352], P(None, 'mp')
- out_master_new: float32 [1536, 768], P('mp', 'dp')
- out_first_new: float32 [1536, 768], P('mp', 'dp')
- out_second_new: float32 [1536, 768], P('mp', 'dp')
- out_weights: bfloat16 [1536, 768], P('mp')
- conv_master_new: float32 [5, 1792], P(None, 'mp')
- conv_first_new: float32 [5, 1792], P(None, 'mp')
- conv_second_new: float32 [5, 1792], P(None, 'mp')
- head_master_new: float32 [24, 67], P('mp')
- head_first_new: float32 [24, 67], P('mp')
- head_second_new: float32 [24, 67], P('mp')
- gain_master_new: float32 [768], replicated
- gain_first_new: float32 [768], replicated
- gain_second_new: float32 [768], replicated
All inputs are finite; a program needn't handle non-finite values.
Results may differ from a plain program's by a relative error of at most 0.0004.
Values may be sent and summed in bfloat16 or wider, within the bound.
No kernel may reach another device: no remote copies, remote signals or barrier semaphores. Data moves between devices by JAX's collectives and lax.ppermute only.
A program may use at most 64 MiB of HBM per device.

v0:
```python
import jax
import jax.numpy as jnp
from jax import lax
from jax.sharding import PartitionSpec as P

beta_one = 0.9
beta_two = 0.95
adam_step = 10
adam_eps = 1e-08
learn_rate = 0.003
max_norm = 1.0


def contract(left, right):
    return lax.dot_general(
        left, right, (((0,), (0,)), ((), ())), preferred_element_type=jnp.float32
    )


def adam_update(gradient, master, first, second, decay):
    first_new = beta_one * first + (1.0 - beta_one) * gradient
    second_new = beta_two * second + (1.0 - beta_two) * gradient * gradient
    ratio = (
        first_new
        / (1.0 - beta_one**adam_step)
        / (jnp.sqrt(second_new / (1.0 - beta_two**adam_step)) + adam_eps)
    )
    return (master - learn_rate * (ratio + decay * master), first_new, second_new)


def body(
    acts,
    proj_cotangent,
    inner_acts,
    out_cotangent,
    in_master,
    in_first,
    in_second,
    out_master,
    out_first,
    out_second,
    conv_grads,
    conv_master,
    conv_first,
    conv_second,
    head_grads,
    head_master,
    head_first,
    head_second,
    gain_grads,
    gain_master,
    gain_first,
    gain_second,
):
    grad_in = lax.psum_scatter(
        contract(acts, proj_cotangent), "dp", scatter_dimension=0, tiled=True
    )
    grad_out = lax.psum_scatter(
        contract(out_cotangent, inner_acts), "dp", scatter_dimension=0, tiled=True
    ).T
    conv_local = jnp.sum(conv_grads, axis=(0, 1))
    head_local = jnp.sum(head_grads, axis=(0, 1))
    grad_conv, grad_head = lax.psum((conv_local, head_local), "dp")
    grad_gain = lax.psum(jnp.sum(gain_grads, axis=(0, 1, 2)), ("dp", "mp"))
    data_first = lax.axis_index("dp") == 0
    model_first = lax.axis_index("mp") == 0
    local_squares = jnp.sum(grad_in * grad_in) + jnp.sum(grad_out * grad_out)
    local_squares = local_squares + jnp.where(
        data_first, jnp.sum(grad_conv * grad_conv) + jnp.sum(grad_head * grad_head), 0.0
    )
    local_squares = local_squares + jnp.where(
        data_first & model_first, jnp.sum(grad_gain * grad_gain), 0.0
    )
    squares = lax.psum(local_squares, ("dp", "mp"))
    clip_factor = jnp.minimum(1.0, max_norm / (jnp.sqrt(squares) + 1e-06))
    new_in = adam_update(clip_factor * grad_in, in_master, in_first, in_second, 0.1)
    new_out = adam_update(clip_factor * grad_out, out_master, out_first, out_second, 0.1)
    new_conv = adam_update(clip_factor * grad_conv, conv_master, conv_first, conv_second, 0.1)
    new_head = adam_update(clip_factor * grad_head, head_master, head_first, head_second, 0.0)
    new_gain = adam_update(clip_factor * grad_gain, gain_master, gain_first, gain_second, 0.0)
    in_weights = lax.all_gather(new_in[0].astype(jnp.bfloat16), "dp", axis=0, tiled=True)
    out_weights = lax.all_gather(new_out[0].astype(jnp.bfloat16), "dp", axis=1, tiled=True)
    return (
        new_in[0],
        new_in[1],
        new_in[2],
        in_weights,
        new_out[0],
        new_out[1],
        new_out[2],
        out_weights,
        new_conv[0],
        new_conv[1],
        new_conv[2],
        new_head[0],
        new_head[1],
        new_head[2],
        new_gain[0],
        new_gain[1],
        new_gain[2],
    )


def solution(mesh):
    return jax.shard_map(
        body,
        mesh=mesh,
        in_specs=(
            P("dp", None),
            P("dp", "mp"),
            P("dp", "mp"),
            P("dp", None),
            P("dp", "mp"),
            P("dp", "mp"),
            P("dp", "mp"),
            P("mp", "dp"),
            P("mp", "dp"),
            P("mp", "dp"),
            P("dp", None, None, "mp"),
            P(None, "mp"),
            P(None, "mp"),
            P(None, "mp"),
            P("dp", None, "mp", None),
            P("mp", None),
            P("mp", None),
            P("mp", None),
            P("dp", None, "mp", None),
            P(),
            P(),
            P(),
        ),
        out_specs=(
            P("dp", "mp"),
            P("dp", "mp"),
            P("dp", "mp"),
            P(None, "mp"),
            P("mp", "dp"),
            P("mp", "dp"),
            P("mp", "dp"),
            P("mp", None),
            P(None, "mp"),
            P(None, "mp"),
            P(None, "mp"),
            P("mp", None),
            P("mp", None),
            P("mp", None),
            P(),
            P(),
            P(),
        ),
        check_vma=False,
    )
```

profile of v0, /device:TPU:1, one launch (start us, length us, event | category | flops | bytes accessed | tf_op | source)
XLA Modules:
  0.0 518.6 jit_solution(9797056187177731817)
XLA Ops:
  7.2 0.0 copy-start
  7.2 0.0 all-reduce.6.cloned.1.call-start
  7.3 1.8 copy-done
  9.1 6.5 %fusion.12 = f32[768,838]{1,0:T(8,128)} fusion(bf16[1792,768]{1,0:T(8,128)(2,1)} %param.22, bf16[1792,838]{0,1:T(8,128)(2,1)S(1)} %copy-done), kind=kOutput, calls=%fused_computation.28 | convolution fusion | flops 2306605056 | bytes 8330240 | tf_op jit(solution)/shard_map/dot_general | solution.py:15
  15.6 0.0 copy-done.1
  15.6 0.0 copy-done.2
  15.6 2.6 fusion.13
  18.2 0.0 copy-start.3
  18.2 0.0 copy-start.4
  18.3 0.0 copy-start.5
  18.3 0.0 copy-start.6
  18.3 0.0 copy-start.7
  18.3 0.0 copy-start.8
  18.3 0.0 all-reduce.6.cloned.1.call-update
  18.3 0.0 copy-start.15
  18.3 0.0 copy-start.16
  18.3 0.0 copy-start.17
  18.4 0.0 copy-start.18
  18.4 0.0 copy-start.19
  18.4 0.0 copy-start.20
  18.4 0.0 copy-start.10
  18.4 0.0 copy-start.11
  18.4 0.0 copy-start.12
  18.4 0.0 all-gather.4.cloned.1.call-start
  18.5 0.4 copy-done.9
  19.0 0.0 copy-done.13
  19.0 250.4 %all-reduce.2 = (f32[5,448]{1,0:T(8,128)S(1)}, f32[6,67]{1,0:T(8,128)S(1)}) all-reduce(f32[5,448]{1,0:T(8,128)S(1)} %reduce_sum.74, f32[6,67]{1,0:T(8,128)S(1)} %reduce_sum.76), channel_id=1, replica_groups=mesh['dp'=64,'mp'=4] {'dp'}, use_global_device_ids=true, to_apply=%region_5.0 | all-reduce | flops 2642 | bytes 21136 | tf_op jit(solution)/shard_map/psum | solution.py:63
  269.4 0.6 multiply_reduce_fusion.4
  270.0 0.6 multiply_reduce_fusion.2
  271.9 0.0 copy-done.14
  272.0 0.0 copy-done.21
  272.0 0.6 dynamic-slice
  273.2 78.6 %psum.30 = f32[768]{0:T(1024)S(1)} all-reduce(f32[768]{0:T(1024)S(1)} %reduce_sum.78), channel_id=1, replica_groups=mesh['dp'=64,'mp'=4] {'dp','mp'}, use_global_device_ids=true, to_apply=%region_11.0 | all-reduce | flops 768 | bytes 6144 | tf_op jit(solution)/shard_map/psum | solution.py:64
  351.8 0.6 multiply_reduce_fusion.3
  353.1 0.0 all-reduce.6.cloned.1.call-done
  353.1 1.5 multiply_reduce_fusion
  354.6 1.4 multiply_reduce_fusion.1
  357.3 73.2 %psum.31 = f32[]{:T(128)} all-reduce(f32[]{:T(128)S(6)} %add.105), channel_id=1, replica_groups=mesh['dp'=64,'mp'=4] {'dp','mp'}, use_global_device_ids=true, to_apply=%region_13.14 | all-reduce | flops 1 | bytes 8 | tf_op jit(solution)/shard_map/psum | solution.py:74
  431.3 0.0 copy-done.3
  431.3 0.0 copy-done.4
  431.3 0.0 copy-done.5
  431.3 1.6 convert_bitcast_fusion
  432.9 0.0 all-gather.4.cloned.1.call-update
  433.0 0.0 copy-done.6
  433.0 0.0 copy-done.7
  433.0 0.0 copy-done.8
  433.0 1.4 convert_bitcast_fusion.1
  434.4 54.2 %all-gather.1 = bf16[64,12,384]{2,1,0:T(8,128)(2,1)} all-gather(bf16[1,12,384]{2,1,0:T(8,128)(2,1)S(1)} %get-tuple-element.81), channel_id=1, replica_groups=mesh['dp'=64,'mp'=4] {'dp'}, dimensions={0}, use_global_device_ids=true | all-gather | bytes 599040 | tf_op jit(solution)/shard_map/all_gather | solution.py:82
  488.7 2.0 reshape.37
  490.7 2.1 copy.44
  492.8 0.0 copy-done.15
  492.8 0.0 copy-done.16
  492.8 0.0 copy-done.17
  492.8 0.6 multiply_subtract_fusion.4
  493.4 0.0 copy-done.18
  493.4 0.0 copy-done.19
  493.4 0.0 copy-done.20
  493.4 0.6 multiply_subtract_fusion.3
  494.0 0.0 copy-done.10
  494.1 0.0 copy-done.12
  494.1 0.6 multiply_subtract_fusion.2
  494.7 10.9 %all-gather.4.cloned.1.call-done = bf16[64,12,838]{2,1,0:T(8,128)(2,1)} async-done(((bf16[1,12,838]{2,1,0:T(8,128)(2,1)}), bf16[64,12,838]{2,1,0:T(8,128)(2,1)}) %all-gather.4.cloned.1.call-update) | async-done | bytes 1287184 | tf_op jit(solution)/shard_map/all_gather | solution.py:81
  505.6 3.7 reshape.35
  509.3 2.5 copy.43
  (10 shorter events, 0.1 us)
Async XLA Ops:
  7.2 1.9 copy-start
  7.2 345.9 %all-reduce.6.cloned.1.call-start = ((), (), s32[]{:S(2)}) async-start(), calls=%async_computation.1 | async-start | bytes 7864320
  9.0 6.5 %copy-start.1 = (bf16[1792,768]{1,0:T(8,128)(2,1)S(1)}, bf16[1792,768]{1,0:T(8,128)(2,1)}, u32[]{:S(2)}) copy-start(bf16[1792,768]{1,0:T(8,128)(2,1)} %param.25) | copy-start | bytes 8257540
  9.0 6.5 %copy-start.2 = (bf16[1792,384]{1,0:T(8,128)(2,1)S(1)}, bf16[1792,384]{1,0:T(8,128)(2,1)}, u32[]{:S(2)}) copy-start(bf16[1792,384]{1,0:T(8,128)(2,1)} %param.24) | copy-start | bytes 4128772
  18.2 0.7 copy-start.9
  18.2 0.8 copy-start.13
  18.2 253.7 %copy-start.14 = (f32[1,2,1,768]{3,2,1,0:T(1,128)S(1)}, f32[1,2,1,768]{3,2,1,0:T(1,128)}, u32[]{:S(2)}) copy-start(f32[1,2,1,768]{3,2,1,0:T(1,128)} %param.40) | copy-start | bytes 18436
  18.2 253.7 %copy-start.21 = (u32[256]{0:T(256)S(1)}, u32[256]{0:T(256)}, u32[]{:S(2)}) copy-start(u32[256]{0:T(256)} %constant.43) | copy-start | bytes 3076
  18.2 413.1 %copy-start.3 = (f32[12,838]{1,0:T(8,128)S(1)}, f32[12,838]{1,0:T(8,128)}, u32[]{:S(2)}) copy-start(f32[12,838]{1,0:T(8,128)} %param.26) | copy-start | bytes 120676
  18.2 413.1 %copy-start.4 = (f32[12,838]{1,0:T(8,128)S(1)}, f32[12,838]{1,0:T(8,128)}, u32[]{:S(2)}) copy-start(f32[12,838]{1,0:T(8,128)} %param.27) | copy-start | bytes 120676
  18.3 413.1 %copy-start.5 = (f32[12,838]{1,0:T(8,128)S(1)}, f32[12,838]{1,0:T(8,128)}, u32[]{:S(2)}) copy-start(f32[12,838]{1,0:T(8,128)} %param.28) | copy-start | bytes 120676
  18.3 414.7 %copy-start.6 = (f32[384,12]{0,1:T(8,128)S(1)}, f32[384,12]{0,1:T(8,128)}, u32[]{:S(2)}) copy-start(f32[384,12]{0,1:T(8,128)} %param.29) | copy-start | bytes 55300
  18.3 414.7 %copy-start.7 = (f32[384,12]{0,1:T(8,128)S(1)}, f32[384,12]{0,1:T(8,128)}, u32[]{:S(2)}) copy-start(f32[384,12]{0,1:T(8,128)} %param.30) | copy-start | bytes 55300
  18.3 414.7 %copy-start.8 = (f32[384,12]{0,1:T(8,128)S(1)}, f32[384,12]{0,1:T(8,128)}, u32[]{:S(2)}) copy-start(f32[384,12]{0,1:T(8,128)} %param.31) | copy-start | bytes 55300
  18.3 474.5 %copy-start.15 = (f32[6,67]{1,0:T(8,128)S(1)}, f32[6,67]{1,0:T(8,128)}, u32[]{:S(2)}) copy-start(f32[6,67]{1,0:T(8,128)} %param.37) | copy-start | bytes 4828
  18.3 474.4 %copy-start.16 = (f32[6,67]{1,0:T(8,128)S(1)}, f32[6,67]{1,0:T(8,128)}, u32[]{:S(2)}) copy-start(f32[6,67]{1,0:T(8,128)} %param.38) | copy-start | bytes 4828
  18.3 474.4 %copy-start.17 = (f32[6,67]{1,0:T(8,128)S(1)}, f32[6,67]{1,0:T(8,128)}, u32[]{:S(2)}) copy-start(f32[6,67]{1,0:T(8,128)} %param.39) | copy-start | bytes 4828
  18.4 475.1 %copy-start.18 = (f32[768]{0:T(1024)S(1)}, f32[768]{0:T(1024)}, u32[]{:S(2)}) copy-start(f32[768]{0:T(1024)} %param.41) | copy-start | bytes 9220
  18.4 475.0 %copy-start.19 = (f32[768]{0:T(1024)S(1)}, f32[768]{0:T(1024)}, u32[]{:S(2)}) copy-start(f32[768]{0:T(1024)} %param.42) | copy-start | bytes 9220
  18.4 475.0 %copy-start.20 = (f32[768]{0:T(1024)S(1)}, f32[768]{0:T(1024)}, u32[]{:S(2)}) copy-start(f32[768]{0:T(1024)} %param.43) | copy-start | bytes 9220
  18.4 475.6 %copy-start.10 = (f32[5,448]{1,0:T(8,128)S(1)}, f32[5,448]{1,0:T(8,128)}, u32[]{:S(2)}) copy-start(f32[5,448]{1,0:T(8,128)} %param.33) | copy-start | bytes 26884
  18.4 475.6 %copy-start.11 = (f32[5,448]{1,0:T(8,128)S(1)}, f32[5,448]{1,0:T(8,128)}, u32[]{:S(2)}) copy-start(f32[5,448]{1,0:T(8,128)} %param.34) | copy-start | bytes 26884
  18.4 475.6 %copy-start.12 = (f32[5,448]{1,0:T(8,128)S(1)}, f32[5,448]{1,0:T(8,128)}, u32[]{:S(2)}) copy-start(f32[5,448]{1,0:T(8,128)} %param.35) | copy-start | bytes 26884
  18.4 487.2 %all-gather.4.cloned.1.call-start = ((), (), s32[]{:S(2)}) async-start(), calls=%async_computation | async-start | bytes 1863680 | tf_op jit(solution)/shard_map/all_gather | solution.py:81
Sparse Core Ops, SparseCore 0:
  18.4 197.3 all-reduce.5
  433.1 72.4 all-gather.3
where the time goes:
time: 519 us
  blocking collectives  457 us (88%)
  between operations  19 us (4%)
  local copies, waits for them, and re-layouts  13.3 us (3%)
  waiting for transfers between devices  11 us (2%)
  other arithmetic  9.66 us (2%)
  matrix products  9.16 us (2%)
    psum x1, blocking collectives, body(): grad_conv, grad_head = lax.psum((conv_local, head_local), 'dp')  250 us
    psum x1, blocking collectives, body(): grad_gain = lax.psum(jnp.sum(gain_grads, axis=(0, 1, 2)), ('dp', 'mp'))  78.6 us
    psum x1, blocking collectives, body(): squares = lax.psum(local_squares, ('dp', 'mp'))  73.2 us
    all_gather x1, blocking collectives, body(): lax.all_gather(new_out[0].astype(jnp.bfloat16), 'dp', axis=1, tiled=True)  54.2 us
    unnamed x49, local copies, waits for them, and re-layouts  13.3 us
    all_gather x1, waiting for transfers between devices, body(): lax.all_gather(new_in[0].astype(jnp.bfloat16), 'dp', axis=0, tiled=True)  10.9 us
  transfers between devices with their start and end apart: 2, of which 1 were waited for; matrix products, arithmetic and copies ran while one was open for 2% of the time, Pallas kernels for 0%

commit v1 on v0

--- a/solution.py
+++ b/solution.py
@@ -52,34 +52,51 @@
     gain_first,
     gain_second,
 ):
-    grad_in = lax.psum_scatter(
-        contract(acts, proj_cotangent), "dp", scatter_dimension=0, tiled=True
-    )
-    grad_out = lax.psum_scatter(
-        contract(out_cotangent, inner_acts), "dp", scatter_dimension=0, tiled=True
-    ).T
+    n_dp = lax.axis_size("dp")
+    width, n_in = acts.shape[1], proj_cotangent.shape[1]
+    rows = width // n_dp
+    part_in = contract(acts, proj_cotangent)
+    part_out = contract(out_cotangent, inner_acts)
+    both = jnp.concatenate([part_in, part_out], axis=1)
+    cols = both.shape[1]
+    both = both.reshape(n_dp, rows, cols)
+    grad_both = lax.psum_scatter(both, "dp", scatter_dimension=0, tiled=True)[0]
+    grad_in = grad_both[:, :n_in]
+    grad_out_t = grad_both[:, n_in:]
+
     conv_local = jnp.sum(conv_grads, axis=(0, 1))
     head_local = jnp.sum(head_grads, axis=(0, 1))
-    grad_conv, grad_head = lax.psum((conv_local, head_local), "dp")
-    grad_gain = lax.psum(jnp.sum(gain_grads, axis=(0, 1, 2)), ("dp", "mp"))
+    gain_local = jnp.sum(gain_grads, axis=(0, 1, 2))
+    n_conv, n_head = conv_local.size, head_local.size
+    small = jnp.concatenate(
+        [conv_local.reshape(-1), head_local.reshape(-1), gain_local]
+    )
+    small = lax.psum(small, "dp")
+    grad_conv = small[:n_conv].reshape(conv_local.shape)
+    grad_head = small[n_conv : n_conv + n_head].reshape(head_local.shape)
+    gain_dp = small[n_conv + n_head :]
+
     data_first = lax.axis_index("dp") == 0
-    model_first = lax.axis_index("mp") == 0
-    local_squares = jnp.sum(grad_in * grad_in) + jnp.sum(grad_out * grad_out)
-    local_squares = local_squares + jnp.where(
-        data_first, jnp.sum(grad_conv * grad_conv) + jnp.sum(grad_head * grad_head), 0.0
-    )
-    local_squares = local_squares + jnp.where(
-        data_first & model_first, jnp.sum(grad_gain * grad_gain), 0.0
-    )
-    squares = lax.psum(local_squares, ("dp", "mp"))
+    local_squares = jnp.sum(grad_in * grad_in) + jnp.sum(grad_out_t * grad_out_t)
+    dp_squares = lax.psum(local_squares, "dp")
+    col_squares = dp_squares + jnp.sum(grad_conv * grad_conv) + jnp.sum(grad_head * grad_head)
+    tail = lax.psum(jnp.concatenate([gain_dp, col_squares[None]]), "mp")
+    grad_gain = tail[:-1]
+    squares = tail[-1] + jnp.sum(grad_gain * grad_gain)
     clip_factor = jnp.minimum(1.0, max_norm / (jnp.sqrt(squares) + 1e-06))
+
     new_in = adam_update(clip_factor * grad_in, in_master, in_first, in_second, 0.1)
-    new_out = adam_update(clip_factor * grad_out, out_master, out_first, out_second, 0.1)
+    new_out = adam_update(clip_factor * grad_out_t.T, out_master, out_first, out_second, 0.1)
     new_conv = adam_update(clip_factor * grad_conv, conv_master, conv_first, conv_second, 0.1)
     new_head = adam_update(clip_factor * grad_head, head_master, head_first, head_second, 0.0)
     new_gain = adam_update(clip_factor * grad_gain, gain_master, gain_first, gain_second, 0.0)
-    in_weights = lax.all_gather(new_in[0].astype(jnp.bfloat16), "dp", axis=0, tiled=True)
-    out_weights = lax.all_gather(new_out[0].astype(jnp.bfloat16), "dp", axis=1, tiled=True)
+
+    low = jnp.concatenate(
+        [new_in[0].astype(jnp.bfloat16), new_out[0].T.astype(jnp.bfloat16)], axis=1
+    )
+    gathered = lax.all_gather(low, "dp", axis=0, tiled=True)
+    in_weights = gathered[:, :n_in]
+    out_weights = gathered[:, n_in:].T
     return (
         new_in[0],
         new_in[1],

time: 519 us -> 543 us (1.046)
  waiting for transfers between devices: 11 us -> 222 us
  blocking collectives: 457 us -> 255 us
  local copies, waits for them, and re-layouts: 13.3 us -> 27.5 us
    psum x3 -> x2, blocking collectives: 402 us -> 255 us  [the longest x1 247 us: body(): dp_squares = lax.psum(local_squares, 'dp')]
    unnamed x3, waiting for transfers between devices: 0.05 us -> 144 us
    all_gather x1, waiting for transfers between devices: 10.9 us -> 78.3 us  [body(): gathered = lax.all_gather(low, 'dp', axis=0, tiled=True)]
    all_gather x1 -> x0, blocking collectives: 54.2 us -> none  [body(): lax.all_gather(new_out[0].astype(jnp.bfloat16), 'dp', axis=1, tiled=True)]
    concatenate x0 -> x2, local copies, waits for them, and re-layouts: none -> 5.59 us  [the longest x1 5.51 us: body(): both = jnp.concatenate([part_in, part_out], axis=1)]
    unnamed x49 -> x45, local copies, waits for them, and re-layouts: 13.3 us -> 11.2 us
  transfers between devices with their start and end apart: 2 -> 2, of which waited for: 1 -> 2; matrix products, arithmetic and copies ran while one was open for 2% -> 0% of each run, Pallas kernels for 0% -> 0%
where the time goes in v1:
time: 543 us; the launch traced here: 542 us
  blocking collectives  255 us (47%)
  waiting for transfers between devices  222 us (41%)
  local copies, waits for them, and re-layouts  27.5 us (5%)
  between operations  18.9 us (3%)
  other arithmetic  12.5 us (2%)
  matrix products  5.84 us (1%)
    psum x1, blocking collectives, body(): dp_squares = lax.psum(local_squares, 'dp')  247 us
    unnamed x3, waiting for transfers between devices  144 us
    all_gather x1, waiting for transfers between devices, body(): gathered = lax.all_gather(low, 'dp', axis=0, tiled=True)  78.3 us
    unnamed x45, local copies, waits for them, and re-layouts  11.2 us
  transfers between devices with their start and end apart: 2, of which 2 were waited for; matrix products, arithmetic and copies ran while one was open for 0% of the time, Pallas kernels for 0%

profile of v1, /device:TPU:1, one launch (start us, length us, event | category | flops | bytes accessed | tf_op | source)
XLA Modules:
  0.0 542.1 jit_solution(3108052154385172136)
XLA Ops:
  7.2 0.0 copy-start
  7.2 0.0 reduce-scatter.4.cloned.1.call-start
  7.3 1.8 copy-done
  9.1 4.6 fusion.13
  13.6 0.0 copy-done.19
  13.6 0.0 copy-done.20
  13.6 1.3 fusion.14
  14.9 2.1 pad_maximum_fusion
  17.0 5.5 %copy.44 = f32[768,1222]{1,0:T(8,128)} copy(f32[768,1222]{0,1:T(8,128)} %pad_maximum_fusion) | data formatting | bytes 7507968 | tf_op jit(solution)/shard_map/concatenate | solution.py:60
  22.5 5.0 reshape.51
  27.5 0.0 copy-start.5
  27.5 0.0 copy-start.6
  27.6 0.0 copy-start.1
  27.6 0.0 copy-start.2
  27.6 0.0 copy-start.3
  27.6 0.0 copy-start.13
  27.6 0.0 copy-start.14
  27.6 0.0 copy-start.15
  27.6 0.0 copy-start.16
  27.6 0.0 copy-start.17
  27.7 0.0 copy-start.18
  27.7 0.0 copy-start.8
  27.7 0.0 copy-start.9
  27.7 0.0 copy-start.10
  27.7 0.0 reduce-scatter.4.cloned.1.call-update
  27.7 0.0 all-gather.3.cloned.1.call-start
  27.8 0.5 copy-done.7
  28.3 0.1 reshape.49
  28.4 0.0 copy-done.11
  28.4 0.1 reshape.50
  28.5 0.1 concatenate.12
  28.6 144.1 %reduce-scatter.4.cloned.1.call-done = f32[1,12,1222]{2,1,0:T(8,128)} async-done(((f32[64,12,1222]{2,1,0:T(8,128)}), f32[1,12,1222]{2,1,0:T(8,128)}) %reduce-scatter.4.cloned.1.call-update) | async-done | bytes 58672
  172.7 1.4 multiply_reduce_fusion
  174.1 1.4 multiply_reduce_fusion.1
  176.8 246.5 %all-reduce.1 = (f32[]{:T(128)}, f32[3410]{0:T(1024)S(1)}) all-reduce(f32[]{:T(128)S(6)} %add.98, f32[3410]{0:T(1024)S(1)} %concatenate.12), channel_id=1, replica_groups=mesh['dp'=64,'mp'=4] {'dp'}, use_global_device_ids=true, to_apply=%region_7.0 | all-reduce | flops 3411 | bytes 27288 | tf_op jit(solution)/shard_map/psum | solution.py:81
  423.4 0.6 multiply_reduce_fusion.2
  424.0 0.7 multiply_reduce_fusion.4
  424.6 0.1 slice.36
  426.7 8.3 %psum.23 = f32[769]{0:T(1024)S(1)} all-reduce(f32[769]{0:T(1024)S(1)} %pad_maximum_fusion.1), channel_id=1, replica_groups=mesh['dp'=64,'mp'=4] {'mp'}, use_global_device_ids=true, to_apply=%region_10.0 | all-reduce | flops 769 | bytes 6152 | tf_op jit(solution)/shard_map/psum | solution.py:83
  435.0 0.5 slice.32
  435.5 0.6 multiply_reduce_fusion.3
  437.5 0.0 copy-done.4
  437.5 0.0 copy-done.5
  437.5 0.0 copy-done.6
  437.5 1.5 convert_bitcast_fusion
  439.0 1.5 fusion.9
  440.5 0.7 maximum_bitcast_fusion
  441.2 0.0 all-gather.3.cloned.1.call-update
  441.2 0.1 slice_multiply_fusion.3
  441.3 0.1 mul.283
  441.4 0.1 mul.269
  441.4 0.0 copy-done.13
  441.4 0.0 copy-done.15
  441.5 0.6 multiply_subtract_fusion.3
  442.1 0.0 copy-done.16
  442.1 0.6 multiply_subtract_fusion.4
  442.7 0.0 copy-done.9
  442.7 0.6 multiply_subtract_fusion.2
  443.4 78.3 %all-gather.3.cloned.1.call-done = bf16[64,12,1222]{2,1,0:T(8,128)(2,1)} async-done(((bf16[1,12,1222]{2,1,0:T(8,128)(2,1)}), bf16[64,12,1222]{2,1,0:T(8,128)(2,1)}) %all-gather.3.cloned.1.call-update) | async-done | bytes 1877008 | tf_op jit(solution)/shard_map/all_gather | solution.py:97
  521.7 4.3 reshape.53
  526.0 2.5 slice.41
  528.5 2.2 slice_bitcast_fusion
  530.7 2.5 copy.45
  533.2 2.1 copy.46
  (20 shorter events, 0.1 us)
Async XLA Ops:
  7.2 1.9 copy-start
  7.2 165.5 %reduce-scatter.4.cloned.1.call-start = ((), (), s32[]{:S(2)}) async-start(), calls=%async_computation.2 | async-start | bytes 5324800
  9.0 4.6 copy-start.19
  9.0 4.6 copy-start.20
  27.5 0.7 copy-start.7
  27.5 0.8 copy-start.11
  27.5 0.9 copy-start.12
  27.5 409.9 %copy-start.4 = (f32[384,12]{0,1:T(8,128)S(1)}, f32[384,12]{0,1:T(8,128)}, u32[]{:S(2)}) copy-start(f32[384,12]{0,1:T(8,128)} %param.29) | copy-start | bytes 55300
  27.5 409.9 %copy-start.5 = (f32[384,12]{0,1:T(8,128)S(1)}, f32[384,12]{0,1:T(8,128)}, u32[]{:S(2)}) copy-start(f32[384,12]{0,1:T(8,128)} %param.30) | copy-start | bytes 55300
  27.5 409.9 %copy-start.6 = (f32[384,12]{0,1:T(8,128)S(1)}, f32[384,12]{0,1:T(8,128)}, u32[]{:S(2)}) copy-start(f32[384,12]{0,1:T(8,128)} %param.31) | copy-start | bytes 55300
  27.6 411.4 %copy-start.1 = (f32[12,838]{1,0:T(8,128)S(1)}, f32[12,838]{1,0:T(8,128)}, u32[]{:S(2)}) copy-start(f32[12,838]{1,0:T(8,128)} %param.26) | copy-start | bytes 120676
  27.6 411.4 %copy-start.2 = (f32[12,838]{1,0:T(8,128)S(1)}, f32[12,838]{1,0:T(8,128)}, u32[]{:S(2)}) copy-start(f32[12,838]{1,0:T(8,128)} %param.27) | copy-start | bytes 120676
  27.6 411.4 %copy-start.3 = (f32[12,838]{1,0:T(8,128)S(1)}, f32[12,838]{1,0:T(8,128)}, u32[]{:S(2)}) copy-start(f32[12,838]{1,0:T(8,128)} %param.28) | copy-start | bytes 120676
  27.6 413.8 %copy-start.13 = (f32[768]{0:T(1024)S(1)}, f32[768]{0:T(1024)}, u32[]{:S(2)}) copy-start(f32[768]{0:T(1024)} %param.41) | copy-start | bytes 9220
  27.6 413.8 %copy-start.14 = (f32[768]{0:T(1024)S(1)}, f32[768]{0:T(1024)}, u32[]{:S(2)}) copy-start(f32[768]{0:T(1024)} %param.42) | copy-start | bytes 9220
  27.6 413.8 %copy-start.15 = (f32[768]{0:T(1024)S(1)}, f32[768]{0:T(1024)}, u32[]{:S(2)}) copy-start(f32[768]{0:T(1024)} %param.43) | copy-start | bytes 9220
  27.6 414.4 %copy-start.16 = (f32[6,67]{1,0:T(8,128)S(1)}, f32[6,67]{1,0:T(8,128)}, u32[]{:S(2)}) copy-start(f32[6,67]{1,0:T(8,128)} %param.37) | copy-start | bytes 4828
  27.6 414.4 %copy-start.17 = (f32[6,67]{1,0:T(8,128)S(1)}, f32[6,67]{1,0:T(8,128)}, u32[]{:S(2)}) copy-start(f32[6,67]{1,0:T(8,128)} %param.38) | copy-start | bytes 4828
  27.7 414.4 %copy-start.18 = (f32[6,67]{1,0:T(8,128)S(1)}, f32[6,67]{1,0:T(8,128)}, u32[]{:S(2)}) copy-start(f32[6,67]{1,0:T(8,128)} %param.39) | copy-start | bytes 4828
  27.7 415.0 %copy-start.8 = (f32[5,448]{1,0:T(8,128)S(1)}, f32[5,448]{1,0:T(8,128)}, u32[]{:S(2)}) copy-start(f32[5,448]{1,0:T(8,128)} %param.33) | copy-start | bytes 26884
  27.7 415.0 %copy-start.9 = (f32[5,448]{1,0:T(8,128)S(1)}, f32[5,448]{1,0:T(8,128)}, u32[]{:S(2)}) copy-start(f32[5,448]{1,0:T(8,128)} %param.34) | copy-start | bytes 26884
  27.7 415.0 %copy-start.10 = (f32[5,448]{1,0:T(8,128)S(1)}, f32[5,448]{1,0:T(8,128)}, u32[]{:S(2)}) copy-start(f32[5,448]{1,0:T(8,128)} %param.35) | copy-start | bytes 26884
  27.7 494.0 %all-gather.3.cloned.1.call-start = ((), (), s32[]{:S(2)}) async-start(), calls=%async_computation.1 | async-start | bytes 2662400 | tf_op jit(solution)/shard_map/all_gather | solution.py:97
Sparse Core Ops, SparseCore 0:
  27.9 144.7 reduce-scatter.3
  441.3 80.3 all-gather.2

commit v2 on v1

--- a/solution.py
+++ b/solution.py
@@ -1,7 +1,7 @@
 import jax
 import jax.numpy as jnp
 from jax import lax
-from jax.sharding import PartitionSpec as P
+from jax.sharding import Mesh, PartitionSpec as P
 
 beta_one = 0.9
 beta_two = 0.95
@@ -28,6 +28,15 @@
     return (master - learn_rate * (ratio + decay * master), first_new, second_new)
 
 
+DP = ("z", "y", "c")
+
+
+def nested_psum(value, axes):
+    for axis in reversed(axes):
+        value = lax.psum(value, axis)
+    return value
+
+
 def body(
     acts,
     proj_cotangent,
@@ -52,7 +61,7 @@
     gain_first,
     gain_second,
 ):
-    n_dp = lax.axis_size("dp")
+    n_dp = lax.axis_size(DP)
     width, n_in = acts.shape[1], proj_cotangent.shape[1]
     rows = width // n_dp
     part_in = contract(acts, proj_cotangent)
@@ -60,7 +69,7 @@
     both = jnp.concatenate([part_in, part_out], axis=1)
     cols = both.shape[1]
     both = both.reshape(n_dp, rows, cols)
-    grad_both = lax.psum_scatter(both, "dp", scatter_dimension=0, tiled=True)[0]
+    grad_both = lax.psum_scatter(both, DP, scatter_dimension=0, tiled=True)[0]
     grad_in = grad_both[:, :n_in]
     grad_out_t = grad_both[:, n_in:]
 
@@ -71,15 +80,17 @@
     small = jnp.concatenate(
         [conv_local.reshape(-1), head_local.reshape(-1), gain_local]
     )
-    small = lax.psum(small, "dp")
+    small = nested_psum(small, DP)
     grad_conv = small[:n_conv].reshape(conv_local.shape)
     grad_head = small[n_conv : n_conv + n_head].reshape(head_local.shape)
     gain_dp = small[n_conv + n_head :]
 
-    data_first = lax.axis_index("dp") == 0
+    data_first = lax.axis_index(DP) == 0
     local_squares = jnp.sum(grad_in * grad_in) + jnp.sum(grad_out_t * grad_out_t)
-    dp_squares = lax.psum(local_squares, "dp")
-    col_squares = dp_squares + jnp.sum(grad_conv * grad_conv) + jnp.sum(grad_head * grad_head)
+    local_squares = local_squares + jnp.where(
+        data_first, jnp.sum(grad_conv * grad_conv) + jnp.sum(grad_head * grad_head), 0.0
+    )
+    col_squares = nested_psum(local_squares, DP)
     tail = lax.psum(jnp.concatenate([gain_dp, col_squares[None]]), "mp")
     grad_gain = tail[:-1]
     squares = tail[-1] + jnp.sum(grad_gain * grad_gain)
@@ -94,7 +105,7 @@
     low = jnp.concatenate(
         [new_in[0].astype(jnp.bfloat16), new_out[0].T.astype(jnp.bfloat16)], axis=1
     )
-    gathered = lax.all_gather(low, "dp", axis=0, tiled=True)
+    gathered = lax.all_gather(low, DP, axis=0, tiled=True)
     in_weights = gathered[:, :n_in]
     out_weights = gathered[:, n_in:].T
     return (
@@ -119,41 +130,43 @@
 
 
 def solution(mesh):
+    n_dp, n_mp = mesh.devices.shape
+    split = Mesh(mesh.devices.reshape(n_dp // 8, 4, 2, n_mp), DP + ("mp",))
     return jax.shard_map(
         body,
-        mesh=mesh,
+        mesh=split,
         in_specs=(
-            P("dp", None),
-            P("dp", "mp"),
-            P("dp", "mp"),
-            P("dp", None),
-            P("dp", "mp"),
-            P("dp", "mp"),
-            P("dp", "mp"),
-            P("mp", "dp"),
-            P("mp", "dp"),
-            P("mp", "dp"),
-            P("dp", None, None, "mp"),
+            P(DP, None),
+            P(DP, "mp"),
+            P(DP, "mp"),
+            P(DP, None),
+            P(DP, "mp"),
+            P(DP, "mp"),
+            P(DP, "mp"),
+            P("mp", DP),
+            P("mp", DP),
+            P("mp", DP),
+            P(DP, None, None, "mp"),
             P(None, "mp"),
             P(None, "mp"),
             P(None, "mp"),
-            P("dp", None, "mp", None),
+            P(DP, None, "mp", None),
             P("mp", None),
             P("mp", None),
             P("mp", None),
-            P("dp", None, "mp", None),
+            P(DP, None, "mp", None),
             P(),
             P(),
             P(),
         ),
         out_specs=(
-            P("dp", "mp"),
-            P("dp", "mp"),
-            P("dp", "mp"),
+            P(DP, "mp"),
+            P(DP, "mp"),
+            P(DP, "mp"),
             P(None, "mp"),
-            P("mp", "dp"),
-            P("mp", "dp"),
-            P("mp", "dp"),
+            P("mp", DP),
+            P("mp", DP),
+            P("mp", DP),
             P("mp", None),
             P(None, "mp"),
             P(None, "mp"),

time: 543 us -> 323 us (0.59)
  blocking collectives: 255 us -> 81.1 us
  waiting for transfers between devices: 222 us -> 177 us
    psum x1 -> x6, blocking collectives: 247 us -> 72.7 us  [nested_psum(): value = lax.psum(value, axis)]
    unnamed x3, waiting for transfers between devices: 144 us -> 97.9 us
    unnamed x45 -> x43, local copies, waits for them, and re-layouts: 11.2 us -> 9.69 us
  transfers between devices with their start and end apart: 2 -> 2, of which waited for: 2 -> 2; matrix products, arithmetic and copies ran while one was open for 0% -> 1% of each run, Pallas kernels for 0% -> 0%
where the time goes in v2:
time: 323 us; the launch traced here: 322 us
  waiting for transfers between devices  177 us (55%)
  blocking collectives  81.1 us (25%)
  local copies, waits for them, and re-layouts  26 us (8%)
  between operations  18.3 us (6%)
  other arithmetic  13.2 us (4%)
  matrix products  6.21 us (2%)
    unnamed x3, waiting for transfers between devices  97.9 us
    all_gather x1, waiting for transfers between devices, body(): gathered = lax.all_gather(low, DP, axis=0, tiled=True)  79.1 us
    psum x6, blocking collectives, nested_psum(): value = lax.psum(value, axis)  72.7 us
    unnamed x43, local copies, waits for them, and re-layouts  9.69 us
    psum x1, blocking collectives, body(): tail = lax.psum(jnp.concatenate([gain_dp, col_squares[None]]), 'mp')  8.39 us
  transfers between devices with their start and end apart: 2, of which 2 were waited for; matrix products, arithmetic and copies ran while one was open for 1% of the time, Pallas kernels for 0%

profile of v2, /device:TPU:1, one launch (start us, length us, event | category | flops | bytes accessed | tf_op | source)
XLA Modules:
  0.0 321.8 jit_solution(5544353051096591747)
XLA Ops:
  7.2 0.0 copy-start
  7.2 0.0 reduce-scatter.4.cloned.1.call-start
  7.3 3.6 %fusion.14 = f32[768,384]{0,1:T(8,128)S(1)} fusion(bf16[1792,768]{1,0:T(8,128)(2,1)} %param.25, bf16[1792,384]{1,0:T(8,128)(2,1)} %param.24), kind=kOutput, calls=%fused_computation.37 | convolution fusion | flops 1056964608 | bytes 5308416 | tf_op jit(solution)/shard_map/dot_general | solution.py:15
  10.9 0.3 copy-done.19
  11.1 2.6 fusion.13
  13.8 2.1 pad_maximum_fusion
  15.8 5.5 %copy.44 = f32[768,1222]{1,0:T(8,128)} copy(f32[768,1222]{0,1:T(8,128)} %pad_maximum_fusion) | data formatting | bytes 7507968 | tf_op jit(solution)/shard_map/concatenate | solution.py:69
  21.3 5.0 %reshape.51 = f32[64,12,1222]{2,1,0:T(8,128)} reshape(f32[768,1222]{1,0:T(8,128)} %copy.44) | data formatting | bytes 7507968 | tf_op jit(solution)/shard_map/reshape | solution.py:71
  26.4 0.0 copy-start.2
  26.4 0.0 copy-start.3
  26.4 0.0 copy-start.4
  26.4 0.0 copy-start.5
  26.4 0.0 copy-start.6
  26.4 0.0 copy-start.13
  26.4 0.0 copy-start.14
  26.5 0.0 copy-start.15
  26.5 0.0 copy-start.16
  26.5 0.0 copy-start.17
  26.5 0.0 copy-start.18
  26.5 0.0 copy-start.8
  26.5 0.0 copy-start.9
  26.5 0.0 copy-start.10
  26.5 0.0 reduce-scatter.4.cloned.1.call-update
  26.6 0.0 all-gather.3.cloned.1.call-start
  26.6 0.5 copy-done.7
  27.1 0.1 reshape.49
  27.2 0.0 copy-done.11
  27.2 0.1 reshape.50
  27.3 0.1 concatenate.12
  27.4 6.4 %psum.49 = f32[3410]{0:T(1024)S(1)} all-reduce(f32[3410]{0:T(1024)S(1)} %concatenate.12), channel_id=1, replica_groups=mesh['z'=8,'y'=4,'c'=2,'mp'=4] {'c'}, use_global_device_ids=true, to_apply=%region_3.0 | all-reduce | flops 3410 | bytes 27280 | tf_op jit(solution)/shard_map/psum | solution.py:36
  33.8 11.7 %psum.50 = f32[3410]{0:T(1024)S(1)} all-reduce(f32[3410]{0:T(1024)S(1)} %psum.49), channel_id=1, replica_groups=mesh['z'=8,'y'=4,'c'=2,'mp'=4] {'y'}, use_global_device_ids=true, to_apply=%region_4.0 | all-reduce | flops 3410 | bytes 27280 | tf_op jit(solution)/shard_map/psum | solution.py:36
  45.5 25.5 %psum.51 = f32[3410]{0:T(1024)S(1)} all-reduce(f32[3410]{0:T(1024)S(1)} %psum.50), channel_id=1, replica_groups=mesh['z'=8,'y'=4,'c'=2,'mp'=4] {'z'}, use_global_device_ids=true, to_apply=%region_5.0 | all-reduce | flops 3410 | bytes 27280 | tf_op jit(solution)/shard_map/psum | solution.py:36
  71.0 0.7 multiply_reduce_fusion.4
  71.7 0.6 multiply_reduce_fusion.2
  73.6 97.8 %reduce-scatter.4.cloned.1.call-done = f32[1,12,1222]{2,1,0:T(8,128)} async-done(((f32[64,12,1222]{2,1,0:T(8,128)}), f32[1,12,1222]{2,1,0:T(8,128)}) %reduce-scatter.4.cloned.1.call-update) | async-done | bytes 58672
  171.4 1.4 multiply_reduce_fusion
  172.9 1.4 multiply_reduce_fusion.1
  175.6 8.7 %psum.52 = f32[]{:T(128)} all-reduce(f32[]{:T(128)S(6)} %add.116), channel_id=1, replica_groups=mesh['z'=8,'y'=4,'c'=2,'mp'=4] {'c'}, use_global_device_ids=true, to_apply=%region_11.12 | all-reduce | flops 1 | bytes 8 | tf_op jit(solution)/shard_map/psum | solution.py:36
  184.3 0.1 slice.36
  184.3 8.1 %psum.53 = f32[]{:T(128)} all-reduce(f32[]{:T(128)} %psum.52), channel_id=1, replica_groups=mesh['z'=8,'y'=4,'c'=2,'mp'=4] {'y'}, use_global_device_ids=true, to_apply=%region_12.13 | all-reduce | flops 1 | bytes 8 | tf_op jit(solution)/shard_map/psum | solution.py:36
  192.5 12.3 %psum.54 = f32[1]{0:T(128)} all-reduce(f32[1]{0:T(128)} %bitcast.1), channel_id=1, replica_groups=mesh['z'=8,'y'=4,'c'=2,'mp'=4] {'z'}, use_global_device_ids=true, to_apply=%region_13.14 | all-reduce | flops 1 | bytes 8 | tf_op jit(solution)/shard_map/psum | solution.py:36
  204.8 0.7 pad_maximum_fusion.1
  205.5 8.4 %psum.55 = f32[769]{0:T(1024)S(1)} all-reduce(f32[769]{0:T(1024)S(1)} %pad_maximum_fusion.1), channel_id=1, replica_groups=mesh['z'=8,'y'=4,'c'=2,'mp'=4] {'mp'}, use_global_device_ids=true, to_apply=%region_14.15 | all-reduce | flops 769 | bytes 6152 | tf_op jit(solution)/shard_map/psum | solution.py:94
  213.9 0.5 slice.32
  214.4 0.6 multiply_reduce_fusion.3
  216.4 1.5 fusion.9
  217.9 0.0 copy-done.4
  217.9 1.5 convert_bitcast_fusion
  219.4 0.7 maximum_bitcast_fusion
  220.1 0.0 all-gather.3.cloned.1.call-update
  220.1 0.1 mul.277
  220.2 0.1 slice_multiply_fusion.3
  220.3 0.1 mul.291
  220.3 0.0 copy-done.13
  220.4 0.6 multiply_subtract_fusion.3
  221.0 0.0 copy-done.17
  221.0 0.6 multiply_subtract_fusion.4
  221.6 0.6 multiply_subtract_fusion.2
  222.3 79.1 %all-gather.3.cloned.1.call-done = bf16[64,12,1222]{2,1,0:T(8,128)(2,1)} async-done(((bf16[1,12,1222]{2,1,0:T(8,128)(2,1)}), bf16[64,12,1222]{2,1,0:T(8,128)(2,1)}) %all-gather.3.cloned.1.call-update) | async-done | bytes 1877008 | tf_op jit(solution)/shard_map/all_gather | solution.py:108
  301.4 4.3 %reshape.53 = bf16[768,1222]{1,0:T(8,128)(2,1)} reshape(bf16[64,12,1222]{2,1,0:T(8,128)(2,1)} %all-gather.3.cloned.1.call-done) | data formatting | bytes 3753984
  305.6 2.5 slice.41
  308.2 2.2 slice_bitcast_fusion
  310.4 2.5 copy.45
  312.9 2.1 copy.46
  (23 shorter events, 0.1 us)
Async XLA Ops:
  7.2 3.7 %copy-start = (bf16[1792,838]{0,1:T(8,128)(2,1)S(1)}, bf16[1792,838]{0,1:T(8,128)(2,1)}, u32[]{:S(2)}) copy-start(bf16[1792,838]{0,1:T(8,128)(2,1)} %param.23) | copy-start | bytes 9010180
  7.2 164.2 %reduce-scatter.4.cloned.1.call-start = ((), (), s32[]{:S(2)}) async-start(), calls=%async_computation.2 | async-start | bytes 5324800
  7.3 3.9 %copy-start.19 = (bf16[1792,768]{1,0:T(8,128)(2,1)S(1)}, bf16[1792,768]{1,0:T(8,128)(2,1)}, u32[]{:S(2)}) copy-start(bf16[1792,768]{1,0:T(8,128)(2,1)} %param.22) | copy-start | bytes 8257540
  26.4 0.7 copy-start.7
  26.4 0.8 copy-start.11
  26.4 0.9 copy-start.12
  26.4 190.0 %copy-start.1 = (f32[12,838]{1,0:T(8,128)S(1)}, f32[12,838]{1,0:T(8,128)}, u32[]{:S(2)}) copy-start(f32[12,838]{1,0:T(8,128)} %param.26) | copy-start | bytes 120676
  26.4 190.0 %copy-start.2 = (f32[12,838]{1,0:T(8,128)S(1)}, f32[12,838]{1,0:T(8,128)}, u32[]{:S(2)}) copy-start(f32[12,838]{1,0:T(8,128)} %param.27) | copy-start | bytes 120676
  26.4 190.0 %copy-start.3 = (f32[12,838]{1,0:T(8,128)S(1)}, f32[12,838]{1,0:T(8,128)}, u32[]{:S(2)}) copy-start(f32[12,838]{1,0:T(8,128)} %param.28) | copy-start | bytes 120676
  26.4 191.5 %copy-start.4 = (f32[384,12]{0,1:T(8,128)S(1)}, f32[384,12]{0,1:T(8,128)}, u32[]{:S(2)}) copy-start(f32[384,12]{0,1:T(8,128)} %param.29) | copy-start | bytes 55300
  26.4 191.5 %copy-start.5 = (f32[384,12]{0,1:T(8,128)S(1)}, f32[384,12]{0,1:T(8,128)}, u32[]{:S(2)}) copy-start(f32[384,12]{0,1:T(8,128)} %param.30) | copy-start | bytes 55300
  26.4 191.5 %copy-start.6 = (f32[384,12]{0,1:T(8,128)S(1)}, f32[384,12]{0,1:T(8,128)}, u32[]{:S(2)}) copy-start(f32[384,12]{0,1:T(8,128)} %param.31) | copy-start | bytes 55300
  26.4 193.9 %copy-start.13 = (f32[768]{0:T(1024)S(1)}, f32[768]{0:T(1024)}, u32[]{:S(2)}) copy-start(f32[768]{0:T(1024)} %param.41) | copy-start | bytes 9220
  26.4 193.9 %copy-start.14 = (f32[768]{0:T(1024)S(1)}, f32[768]{0:T(1024)}, u32[]{:S(2)}) copy-start(f32[768]{0:T(1024)} %param.42) | copy-start | bytes 9220
  26.5 193.9 %copy-start.15 = (f32[768]{0:T(1024)S(1)}, f32[768]{0:T(1024)}, u32[]{:S(2)}) copy-start(f32[768]{0:T(1024)} %param.43) | copy-start | bytes 9220
  26.5 194.5 %copy-start.16 = (f32[6,67]{1,0:T(8,128)S(1)}, f32[6,67]{1,0:T(8,128)}, u32[]{:S(2)}) copy-start(f32[6,67]{1,0:T(8,128)} %param.37) | copy-start | bytes 4828
  26.5 194.5 %copy-start.17 = (f32[6,67]{1,0:T(8,128)S(1)}, f32[6,67]{1,0:T(8,128)}, u32[]{:S(2)}) copy-start(f32[6,67]{1,0:T(8,128)} %param.38) | copy-start | bytes 4828
  26.5 194.5 %copy-start.18 = (f32[6,67]{1,0:T(8,128)S(1)}, f32[6,67]{1,0:T(8,128)}, u32[]{:S(2)}) copy-start(f32[6,67]{1,0:T(8,128)} %param.39) | copy-start | bytes 4828
  26.5 195.1 %copy-start.8 = (f32[5,448]{1,0:T(8,128)S(1)}, f32[5,448]{1,0:T(8,128)}, u32[]{:S(2)}) copy-start(f32[5,448]{1,0:T(8,128)} %param.33) | copy-start | bytes 26884
  26.5 195.1 %copy-start.9 = (f32[5,448]{1,0:T(8,128)S(1)}, f32[5,448]{1,0:T(8,128)}, u32[]{:S(2)}) copy-start(f32[5,448]{1,0:T(8,128)} %param.34) | copy-start | bytes 26884
  26.5 195.1 %copy-start.10 = (f32[5,448]{1,0:T(8,128)S(1)}, f32[5,448]{1,0:T(8,128)}, u32[]{:S(2)}) copy-start(f32[5,448]{1,0:T(8,128)} %param.35) | copy-start | bytes 26884
  26.6 274.8 %all-gather.3.cloned.1.call-start = ((), (), s32[]{:S(2)}) async-start(), calls=%async_computation.1 | async-start | bytes 2662400 | tf_op jit(solution)/shard_map/all_gather | solution.py:108
Sparse Core Ops, SparseCore 0:
  26.7 144.6 reduce-scatter.3
  220.2 81.0 all-gather.2

commit v3 on v2

--- a/solution.py
+++ b/solution.py
@@ -37,6 +37,17 @@
     return value
 
 
+def scatter_sum(value, axis):
+    n = lax.axis_size(axis)
+    me = lax.axis_index(axis)
+    total = lax.dynamic_index_in_dim(value, me, 0, keepdims=False)
+    for shift in range(1, n):
+        part = lax.dynamic_index_in_dim(value, (me + shift) % n, 0, keepdims=False)
+        pairs = [(j, (j + shift) % n) for j in range(n)]
+        total = total + lax.ppermute(part, axis, pairs)
+    return total
+
+
 def body(
     acts,
     proj_cotangent,
@@ -66,10 +77,15 @@
     rows = width // n_dp
     part_in = contract(acts, proj_cotangent)
     part_out = contract(out_cotangent, inner_acts)
-    both = jnp.concatenate([part_in, part_out], axis=1)
-    cols = both.shape[1]
-    both = both.reshape(n_dp, rows, cols)
-    grad_both = lax.psum_scatter(both, DP, scatter_dimension=0, tiled=True)[0]
+    sizes = [lax.axis_size(a) for a in DP]
+    both = jnp.concatenate(
+        [part_in.reshape(*sizes, rows, -1), part_out.reshape(*sizes, rows, -1)], axis=-1
+    )
+    both = jnp.moveaxis(both, 2, 0)
+    both = scatter_sum(both, DP[2])
+    both = jnp.moveaxis(both, 1, 0)
+    both = scatter_sum(both, DP[1])
+    grad_both = scatter_sum(both, DP[0])
     grad_in = grad_both[:, :n_in]
     grad_out_t = grad_both[:, n_in:]
 

time: 323 us -> 281 us (0.87)
  waiting for transfers between devices: 177 us -> 84.7 us
  starting transfers between devices: 0.08 us -> 18.6 us
  blocking collectives: 81.1 us -> 96.7 us
  other arithmetic: 13.2 us -> 22.1 us
  matrix products: 6.21 us -> 11.2 us
    unnamed x3 -> x1, waiting for transfers between devices: 97.9 us -> 0.02 us
    ppermute x0 -> x11, starting transfers between devices: none -> 18.6 us  [scatter_sum(): total = total + lax.ppermute(part, axis, pairs)]
    psum x6, blocking collectives: 72.7 us -> 88.2 us  [nested_psum(): value = lax.psum(value, axis)]
    ppermute x0 -> x11, waiting for transfers between devices: none -> 7.25 us  [scatter_sum(): total = total + lax.ppermute(part, axis, pairs)]
    add x0 -> x3, other arithmetic: none -> 6.29 us  [scatter_sum(): total = total + lax.ppermute(part, axis, pairs)]
    concatenate x1 -> x0, local copies, waits for them, and re-layouts: 5.51 us -> none  [body(): both = jnp.concatenate([part_in, part_out], axis=1)]
    dot_general x2, matrix products: 6.21 us -> 11.2 us  [contract(): lax.dot_general(left, right, (((0,), (0,)), ((), ())), preferred_element_...]
    unnamed x43 -> x32, local copies, waits for them, and re-layouts: 9.69 us -> 12 us
  transfers between devices with their start and end apart: 2 -> 12, of which waited for: 2 -> 4; matrix products, arithmetic and copies ran while one was open for 1% -> 2% of each run, Pallas kernels for 0% -> 0%
where the time goes in v3:
time: 281 us; the launch traced here: 280 us
  blocking collectives  96.7 us (34%)
  waiting for transfers between devices  84.7 us (30%)
  local copies, waits for them, and re-layouts  28.3 us (10%)
  other arithmetic  22.1 us (8%)
  starting transfers between devices  18.6 us (7%)
  between operations  18.3 us (7%)
  matrix products  11.2 us (4%)
    psum x6, blocking collectives, nested_psum(): value = lax.psum(value, axis)  88.2 us
    all_gather x1, waiting for transfers between devices, body(): gathered = lax.all_gather(low, DP, axis=0, tiled=True)  77.5 us
    ppermute x11, starting transfers between devices, scatter_sum(): total = total + lax.ppermute(part, axis, pairs)  18.6 us
    unnamed x32, local copies, waits for them, and re-layouts  12 us
    dot_general x2, matrix products, contract(): lax.dot_general(left, right, (((0,), (0,)), ((), ())), preferred_element_...  11.2 us
    psum x1, blocking collectives, body(): tail = lax.psum(jnp.concatenate([gain_dp, col_squares[None]]), 'mp')  8.48 us
    ppermute x11, waiting for transfers between devices, scatter_sum(): total = total + lax.ppermute(part, axis, pairs)  7.25 us
    add x3, other arithmetic, scatter_sum(): total = total + lax.ppermute(part, axis, pairs)  6.29 us
  transfers between devices with their start and end apart: 12, of which 4 were waited for; matrix products, arithmetic and copies ran while one was open for 2% of the time, Pallas kernels for 0%

profile of v3, /device:TPU:1, one launch (start us, length us, event | category | flops | bytes accessed | tf_op | source)
XLA Modules:
  0.0 279.9 jit_solution(11341371203019863444)
XLA Ops:
  7.2 0.0 copy-start
  7.2 0.0 all-gather.3.cloned.1.call-start
  7.3 1.8 copy-done
  9.0 6.4 %fusion.23 = f32[768,838]{1,0:T(8,128)} fusion(bf16[1792,768]{1,0:T(8,128)(2,1)} %param.22, bf16[1792,838]{0,1:T(8,128)(2,1)S(1)} %copy-done), kind=kOutput, calls=%fused_computation.71 | convolution fusion | flops 2306605056 | bytes 8330240 | tf_op jit(solution)/shard_map/dot_general | solution.py:15
  15.4 4.3 %reshape.66 = f32[8,4,2,12,838]{4,3,2,1,0:T(8,128)} reshape(f32[768,838]{1,0:T(8,128)} %fusion.23) | data formatting | bytes 5148672 | tf_op jit(solution)/shard_map/reshape | solution.py:82
  19.7 4.8 %fusion.24 = f32[768,384]{1,0:T(8,128)} fusion(bf16[1792,768]{1,0:T(8,128)(2,1)} %param.25, bf16[1792,384]{1,0:T(8,128)(2,1)} %param.24), kind=kOutput, calls=%fused_computation.72 | convolution fusion | flops 1056964608 | bytes 5308416 | tf_op jit(solution)/shard_map/dot_general | solution.py:15
  24.5 2.4 reshape.67
  26.9 4.8 %fusion.1 = (f32[8,4,1,12,1222]{4,3,2,1,0:T(8,128)}, f32[8,4,1,12,1222]{4,3,2,1,0:T(8,128)S(1)}) fusion(s32[]{:T(128)S(6)} %select_n.96, f32[8,4,2,12,838]{4,3,2,1,0:T(8,128)} %reshape.66, f32[8,4,2,12,384]{4,3,2,1,0:T(8,128)} %reshape.67, s32[]{:T(128)S(6)} %select_n.98), kind=kLoop, calls=%fused_computation.5 | loop fusion | flops 938496 | bytes 7507976 | tf_op jit(solution)/shard_map/concatenate | solution.py:81
  31.7 2.4 copy.75
  34.1 3.2 %collective-permute-start = (f32[8,4,12,1222]{3,0,2,1:T(8,128)}, f32[8,4,12,1222]{3,0,2,1:T(8,128)}, u32[]{:S(2)}, u32[]{:S(2)}) collective-permute-start(f32[8,4,12,1222]{3,0,2,1:T(8,128)} %bitcast.63), channel_id=1, source_target_pairs={{0,4},{4,0},{1,5},{5,1},{2,6},{6,2},{3,7},{7,3},{8,12},{12,8},{9,1... | collective-permute-start | bytes 5630984 | tf_op jit(solution)/shard_map/ppermute | solution.py:47
  37.3 3.9 %collective-permute-done = f32[8,4,12,1222]{3,0,2,1:T(8,128)} collective-permute-done((f32[8,4,12,1222]{3,0,2,1:T(8,128)}, f32[8,4,12,1222]{3,0,2,1:T(8,128)}, u32[]{:S(2)}, u32[]{:S(2)}) %collective-permute-start) | collective-permute-done | bytes 1877024 | tf_op jit(solution)/shard_map/ppermute | solution.py:47
  41.2 3.5 %bitcast_add_fusion = f32[8,4,12,1222]{3,0,2,1:T(8,128)S(1)} fusion(f32[8,4,12,1222]{3,0,2,1:T(8,128)} %collective-permute-done, f32[8,4,1,12,1222]{4,3,2,1,0:T(8,128)} %get-tuple-element.85), kind=kLoop, calls=%fused_computation.6 | loop fusion | flops 469248 | bytes 5630976 | tf_op jit(solution)/shard_map/add | solution.py:47
  44.8 1.3 copy-done.1
  46.1 1.1 dynamic-slice_bitcast_fusion.2
  47.1 2.2 collective-permute-start.2
  49.3 1.1 collective-permute-start.3
  50.5 0.1 reshape.64
  50.5 0.1 reshape.65
  50.7 0.1 concatenate.12
  50.8 4.4 %psum.49 = f32[3410]{0:T(1024)S(1)} all-reduce(f32[3410]{0:T(1024)S(1)} %concatenate.12), channel_id=1, replica_groups=mesh['z'=8,'y'=4,'c'=2,'mp'=4] {'c'}, use_global_device_ids=true, to_apply=%region_3.4 | all-reduce | flops 3410 | bytes 27280 | tf_op jit(solution)/shard_map/psum | solution.py:36
  55.2 25.9 %psum.50 = f32[3410]{0:T(1024)S(1)} all-reduce(f32[3410]{0:T(1024)S(1)} %psum.49), channel_id=1, replica_groups=mesh['z'=8,'y'=4,'c'=2,'mp'=4] {'y'}, use_global_device_ids=true, to_apply=%region_4.5 | all-reduce | flops 3410 | bytes 27280 | tf_op jit(solution)/shard_map/psum | solution.py:36
  81.1 23.9 %psum.51 = f32[3410]{0:T(1024)S(1)} all-reduce(f32[3410]{0:T(1024)S(1)} %psum.50), channel_id=1, replica_groups=mesh['z'=8,'y'=4,'c'=2,'mp'=4] {'z'}, use_global_device_ids=true, to_apply=%region_5.6 | all-reduce | flops 3410 | bytes 27280 | tf_op jit(solution)/shard_map/psum | solution.py:36
  104.9 0.0 collective-permute-done.1
  105.0 0.0 collective-permute-done.2
  105.0 1.6 fusion.3
  106.6 0.4 constant_dynamic-slice_fusion.7
  106.9 0.3 collective-permute-start.10
  107.2 1.5 collective-permute-start.4
  108.7 0.6 multiply_reduce_fusion.2
  109.4 2.1 collective-permute-start.6
  111.5 3.4 %collective-permute-start.7 = (f32[12,1222]{1,0:T(8,128)S(1)}, f32[12,1222]{1,0:T(8,128)}, u32[]{:S(2)}, u32[]{:S(2)}) collective-permute-start(f32[12,1222]{1,0:T(8,128)S(1)} %bitcast.73), channel_id=1, source_target_pairs={{0,128},{32,160},{64,192},{96,224},{128,0},{160,32},{192,64},{224,... | collective-permute-start | bytes 175976 | tf_op jit(solution)/shard_map/ppermute | solution.py:47
  114.9 0.0 copy-start.2
  115.0 1.3 collective-permute-start.8
  116.2 3.6 %collective-permute-start.9 = (f32[12,1222]{1,0:T(8,128)S(1)}, f32[12,1222]{1,0:T(8,128)}, u32[]{:S(2)}, u32[]{:S(2)}) collective-permute-start(f32[12,1222]{1,0:T(8,128)S(1)} %bitcast.74), channel_id=1, source_target_pairs={{0,192},{32,224},{64,0},{96,32},{128,64},{160,96},{192,128},{224,1... | collective-permute-start | bytes 175976 | tf_op jit(solution)/shard_map/ppermute | solution.py:47
  119.8 0.7 multiply_reduce_fusion.4
  121.8 1.1 collective-permute-done.8
  122.8 2.2 collective-permute-done.9
  125.1 1.2 fusion.9
  126.2 0.6 multiply_reduce_fusion
  126.8 0.7 multiply_reduce_fusion.1
  128.8 14.5 %psum.52 = f32[]{:T(128)} all-reduce(f32[]{:T(128)S(6)} %add.306), channel_id=1, replica_groups=mesh['z'=8,'y'=4,'c'=2,'mp'=4] {'c'}, use_global_device_ids=true, to_apply=%region_10.11 | all-reduce | flops 1 | bytes 8 | tf_op jit(solution)/shard_map/psum | solution.py:36
  143.3 0.1 slice.36
  143.4 6.7 %psum.53 = f32[]{:T(128)} all-reduce(f32[]{:T(128)} %psum.52), channel_id=1, replica_groups=mesh['z'=8,'y'=4,'c'=2,'mp'=4] {'y'}, use_global_device_ids=true, to_apply=%region_11.12 | all-reduce | flops 1 | bytes 8 | tf_op jit(solution)/shard_map/psum | solution.py:36
  150.1 12.8 %psum.54 = f32[1]{0:T(128)} all-reduce(f32[1]{0:T(128)} %bitcast.6), channel_id=1, replica_groups=mesh['z'=8,'y'=4,'c'=2,'mp'=4] {'z'}, use_global_device_ids=true, to_apply=%region_12.13 | all-reduce | flops 1 | bytes 8 | tf_op jit(solution)/shard_map/psum | solution.py:36
  162.9 0.7 pad_maximum_fusion
  163.6 8.5 %psum.55 = f32[769]{0:T(1024)S(1)} all-reduce(f32[769]{0:T(1024)S(1)} %pad_maximum_fusion), channel_id=1, replica_groups=mesh['z'=8,'y'=4,'c'=2,'mp'=4] {'mp'}, use_global_device_ids=true, to_apply=%region_13.14 | all-reduce | flops 769 | bytes 6152 | tf_op jit(solution)/shard_map/psum | solution.py:110
  172.1 0.5 slice.32
  172.6 0.6 multiply_reduce_fusion.3
  174.6 1.5 convert_bitcast_fusion
  176.0 1.6 fusion.19
  177.6 0.7 maximum_bitcast_fusion
  178.3 0.0 all-gather.3.cloned.1.call-update
  178.3 0.1 mul.277
  178.4 0.1 slice_multiply_fusion.3
  178.5 0.1 mul.291
  178.6 0.6 multiply_subtract_fusion.3
  179.2 1.3 multiply_subtract_fusion.4
  180.5 1.4 multiply_subtract_fusion.2
  181.9 77.5 %all-gather.3.cloned.1.call-done = bf16[64,12,1222]{2,1,0:T(8,128)(2,1)} async-done(((bf16[1,12,1222]{2,1,0:T(8,128)(2,1)}), bf16[64,12,1222]{2,1,0:T(8,128)(2,1)}) %all-gather.3.cloned.1.call-update) | async-done | bytes 1877008 | tf_op jit(solution)/shard_map/all_gather | solution.py:124
  259.4 4.3 %reshape.69 = bf16[768,1222]{1,0:T(8,128)(2,1)} reshape(bf16[64,12,1222]{2,1,0:T(8,128)(2,1)} %all-gather.3.cloned.1.call-done) | data formatting | bytes 3753984
  263.7 2.5 slice.41
  266.2 2.2 slice_bitcast_fusion
  268.4 2.5 copy.54
  270.9 2.1 copy.55
  (37 shorter events, 0.2 us)
Async XLA Ops:
  7.2 1.9 copy-start
  7.2 252.2 %all-gather.3.cloned.1.call-start = ((), (), s32[]{:S(2)}) async-start(), calls=%async_computation | async-start | bytes 2662400 | tf_op jit(solution)/shard_map/all_gather | solution.py:124
  34.1 7.1 %collective-permute-start = (f32[8,4,12,1222]{3,0,2,1:T(8,128)}, f32[8,4,12,1222]{3,0,2,1:T(8,128)}, u32[]{:S(2)}, u32[]{:S(2)}) collective-permute-start(f32[8,4,12,1222]{3,0,2,1:T(8,128)} %bitcast.63), channel_id=1, source_target_pairs={{0,4},{4,0},{1,5},{5,1},{2,6},{6,2},{3,7},{7,3},{8,12},{12,8},{9,1... | collective-permute-start | bytes 5630984 | tf_op jit(solution)/shard_map/ppermute | solution.py:47
  44.8 1.3 copy-start.1
  46.1 4.3 %copy-start.5 = (f32[1,2,5,448]{3,1,2,0:T(2,128)S(1)}, f32[1,2,5,448]{3,1,2,0:T(2,128)}, u32[]{:S(2)}) copy-start(f32[1,2,5,448]{3,1,2,0:T(2,128)} %param.32) | copy-start | bytes 53764
  46.1 4.5 %copy-start.6 = (f32[1,2,6,67]{3,1,2,0:T(2,128)S(1)}, f32[1,2,6,67]{3,1,2,0:T(2,128)}, u32[]{:S(2)}) copy-start(f32[1,2,6,67]{3,1,2,0:T(2,128)} %param.36) | copy-start | bytes 9652
  46.1 4.5 %copy-start.7 = (f32[1,2,1,768]{3,2,1,0:T(1,128)S(1)}, f32[1,2,1,768]{3,2,1,0:T(1,128)}, u32[]{:S(2)}) copy-start(f32[1,2,1,768]{3,2,1,0:T(1,128)} %param.40) | copy-start | bytes 18436
  47.1 57.8 %collective-permute-start.1 = (f32[8,12,1222]{2,0,1:T(8,128)}, f32[8,12,1222]{2,0,1:T(8,128)}, u32[]{:S(2)}, u32[]{:S(2)}) collective-permute-start(f32[8,12,1222]{2,0,1:T(8,128)} %get-tuple-element.87), channel_id=1, source_target_pairs={{0,8},{8,16},{16,24},{24,0},{1,9},{9,17},{17,25},{25,1},{2,10},{10... | collective-permute-start | bytes 1407752 | tf_op jit(solution)/shard_map/ppermute | solution.py:47
  47.1 57.8 %collective-permute-start.2 = (f32[8,12,1222]{2,0,1:T(8,128)}, f32[8,12,1222]{2,0,1:T(8,128)}, u32[]{:S(2)}, u32[]{:S(2)}) collective-permute-start(f32[8,12,1222]{2,0,1:T(8,128)} %get-tuple-element.89), channel_id=1, source_target_pairs={{0,16},{8,24},{16,0},{24,8},{1,17},{9,25},{17,1},{25,9},{2,18},{10... | collective-permute-start | bytes 1407752 | tf_op jit(solution)/shard_map/ppermute | solution.py:47
  49.3 55.6 %collective-permute-start.3 = (f32[8,12,1222]{2,0,1:T(8,128)S(1)}, f32[8,12,1222]{2,0,1:T(8,128)}, u32[]{:S(2)}, u32[]{:S(2)}) collective-permute-start(f32[8,12,1222]{2,0,1:T(8,128)S(1)} %get-tuple-element.88), channel_id=1, source_target_pairs={{0,24},{8,0},{16,8},{24,16},{1,25},{9,1},{17,9},{25,17},{2,26},{10... | collective-permute-start | bytes 1407752 | tf_op jit(solution)/shard_map/ppermute | solution.py:47
  104.9 69.6 %copy-start.4 = (f32[384,12]{0,1:T(8,128)S(1)}, f32[384,12]{0,1:T(8,128)}, u32[]{:S(2)}) copy-start(f32[384,12]{0,1:T(8,128)} %param.29) | copy-start | bytes 55300
  104.9 73.6 %copy-start.8 = (f32[768]{0:T(1024)S(1)}, f32[768]{0:T(1024)}, u32[]{:S(2)}) copy-start(f32[768]{0:T(1024)} %param.41) | copy-start | bytes 9220
  104.9 73.6 %copy-start.9 = (f32[768]{0:T(1024)S(1)}, f32[768]{0:T(1024)}, u32[]{:S(2)}) copy-start(f32[768]{0:T(1024)} %param.42) | copy-start | bytes 9220
  104.9 73.6 %copy-start.10 = (f32[768]{0:T(1024)S(1)}, f32[768]{0:T(1024)}, u32[]{:S(2)}) copy-start(f32[768]{0:T(1024)} %param.43) | copy-start | bytes 9220
  106.9 8.0 %collective-permute-start.10 = (f32[12,1222]{1,0:T(8,128)S(1)}, f32[12,1222]{1,0:T(8,128)S(1)}, u32[]{:S(2)}, u32[]{:S(2)}) collective-permute-start(f32[12,1222]{1,0:T(8,128)S(1)} %bitcast.77), channel_id=1, source_target_pairs={{0,224},{32,0},{64,32},{96,64},{128,96},{160,128},{192,160},{224,1... | collective-permute-start | bytes 175976 | tf_op jit(solution)/shard_map/ppermute | solution.py:47
  107.2 9.0 %collective-permute-start.4 = (f32[12,1222]{1,0:T(8,128)S(1)}, f32[12,1222]{1,0:T(8,128)S(1)}, u32[]{:S(2)}, u32[]{:S(2)}) collective-permute-start(f32[12,1222]{1,0:T(8,128)S(1)} %bitcast.76), channel_id=1, source_target_pairs={{0,32},{32,64},{64,96},{96,128},{128,160},{160,192},{192,224},{224... | collective-permute-start | bytes 175976 | tf_op jit(solution)/shard_map/ppermute | solution.py:47
  109.3 12.4 %collective-permute-start.5 = (f32[12,1222]{1,0:T(8,128)S(1)}, f32[12,1222]{1,0:T(8,128)}, u32[]{:S(2)}, u32[]{:S(2)}) collective-permute-start(f32[12,1222]{1,0:T(8,128)S(1)} %bitcast.71), channel_id=1, source_target_pairs={{0,64},{32,96},{64,128},{96,160},{128,192},{160,224},{192,0},{224,... | collective-permute-start | bytes 175976 | tf_op jit(solution)/shard_map/ppermute | solution.py:47
  109.4 12.4 %collective-permute-start.6 = (f32[12,1222]{1,0:T(8,128)S(1)}, f32[12,1222]{1,0:T(8,128)}, u32[]{:S(2)}, u32[]{:S(2)}) collective-permute-start(f32[12,1222]{1,0:T(8,128)S(1)} %bitcast.72), channel_id=1, source_target_pairs={{0,96},{32,128},{64,160},{96,192},{128,224},{160,0},{192,32},{224,... | collective-permute-start | bytes 175976 | tf_op jit(solution)/shard_map/ppermute | solution.py:47
  111.5 10.2 %collective-permute-start.7 = (f32[12,1222]{1,0:T(8,128)S(1)}, f32[12,1222]{1,0:T(8,128)}, u32[]{:S(2)}, u32[]{:S(2)}) collective-permute-start(f32[12,1222]{1,0:T(8,128)S(1)} %bitcast.73), channel_id=1, source_target_pairs={{0,128},{32,160},{64,192},{96,224},{128,0},{160,32},{192,64},{224,... | collective-permute-start | bytes 175976 | tf_op jit(solution)/shard_map/ppermute | solution.py:47
  114.9 4.8 %copy-start.2 = (f32[12,1222]{1,0:T(8,128)}, f32[12,1222]{1,0:T(8,128)S(1)}, u32[]{:S(2)}) copy-start(f32[12,1222]{1,0:T(8,128)S(1)} %collective-permute-done.10) | copy-start | bytes 175972
  115.0 7.9 %collective-permute-start.8 = (f32[12,1222]{1,0:T(8,128)S(1)}, f32[12,1222]{1,0:T(8,128)}, u32[]{:S(2)}, u32[]{:S(2)}) collective-permute-start(f32[12,1222]{1,0:T(8,128)S(1)} %bitcast.75), channel_id=1, source_target_pairs={{0,160},{32,192},{64,224},{96,0},{128,32},{160,64},{192,96},{224,1... | collective-permute-start | bytes 175976 | tf_op jit(solution)/shard_map/ppermute | solution.py:47
  116.2 3.6 %copy-start.3 = (f32[12,1222]{1,0:T(8,128)}, f32[12,1222]{1,0:T(8,128)S(1)}, u32[]{:S(2)}) copy-start(f32[12,1222]{1,0:T(8,128)S(1)} %collective-permute-done.4) | copy-start | bytes 175972
  116.2 8.8 %collective-permute-start.9 = (f32[12,1222]{1,0:T(8,128)S(1)}, f32[12,1222]{1,0:T(8,128)}, u32[]{:S(2)}, u32[]{:S(2)}) collective-permute-start(f32[12,1222]{1,0:T(8,128)S(1)} %bitcast.74), channel_id=1, source_target_pairs={{0,192},{32,224},{64,0},{96,32},{128,64},{160,96},{192,128},{224,1... | collective-permute-start | bytes 175976 | tf_op jit(solution)/shard_map/ppermute | solution.py:47
Sparse Core Ops, SparseCore 0:
  178.4 80.9 all-gather.2
